TPU v7x, 32 devices: a whole 2x2x4 slice. The times are simulated.
32 devices in a mesh: groups: 2 (over y), feat: 4 (over z), tower: 4 (over x, core).
Axes of the slice: x: 2, y: 2, z: 4, core: 2. Of those that a mesh axis runs over, the one named last changes fastest.
Arguments:
- pooled_first: bfloat16 [4, 16, 3072, 128], P('tower', 'feat', 'groups'), parts along dimension 2, may hold values from -6 to 6
- pooled_second: bfloat16 [4, 16, 3072, 128], P('tower', 'feat', 'groups'), parts along dimension 2, may hold values from -6 to 6
- feature_order: int32 [4, 32], P('tower'), may hold values from 0 to 31, each once within a row
- cross_down: bfloat16 [4, 4096, 256], P('tower', 'feat'), may hold values from -0.09375 to 0.09375
- cross_up: bfloat16 [4, 4096, 256], P('tower', 'feat'), may hold values from -0.375 to 0.375
- cross_bias: float32 [4, 4096], P('tower'), may hold values from -3 to 3
- compress_weight: bfloat16 [4, 4096, 512], P('tower', 'feat'), may hold values from -0.09375 to 0.09375
- compress_bias: float32 [4, 512], P('tower'), may hold values from -3 to 3
- dense_vector: bfloat16 [3072, 128], P(('groups', 'feat', 'tower')), parts along dimension 0, may hold values from -6 to 6
- mlp_weight: bfloat16 [248, 1024], P('tower'), may hold values from -0.375 to 0.375
- mlp_bias: float32 [1024], replicated, may hold values from -3 to 3
Outputs:
- top_hidden: bfloat16 [3072, 1024], P(('groups', 'feat', 'tower')), parts along dimension 0
There are 2 independent parts, one for each index of `groups`. A program takes and returns all parts, laid end to end along the dimension named above; an argument that names none is the same for every part. Nothing has to cross between parts.
Inputs may be any that keep to these rules, and one draw needn't show every extreme that they name: Each row of feature_order names every number from 0 to 31 once.
All inputs are finite; a program needn't handle non-finite values.
Results may differ from a plain program's by a relative error of at most 0.0072.
Values may be sent and summed in bfloat16 or wider, within the bound.
No kernel may reach another device: no remote copies, remote signals or barrier semaphores. Data moves between devices by JAX's collectives and lax.ppermute only.
A program may use at most 64 MiB of HBM per device.

v0:
```python
import functools
import math
import jax
import jax.numpy as jnp
import numpy as np
from jax import lax
from jax.sharding import PartitionSpec as P


def pair_positions(vector_count):
    upper_rows, upper_cols = np.triu_indices(vector_count, 1)
    return upper_rows * vector_count + upper_cols


def received_feature_table(rows_here, feat_count, group_count, entry_count):
    piece = rows_here // group_count
    table = np.zeros((group_count, group_count, feat_count * piece // entry_count), np.int32)
    for group in range(group_count):
        for shift in range(group_count):
            source = (group - shift) % group_count
            blocks = []
            for owner in range(feat_count):
                start = owner * rows_here + source * piece
                blocks.extend(range(start // entry_count, (start + piece) // entry_count))
            table[group, shift] = blocks
    return table


def gather_rows(part, group_count):
    own = lax.all_gather(part, "feat", axis=0, tiled=True)
    received = [own]
    for shift in range(1, group_count):
        pairs = [(source, (source + shift) % group_count) for source in range(group_count)]
        received.append(lax.ppermute(own, "groups", pairs))
    return received


def on_device(
    pooled_first,
    pooled_second,
    feature_order,
    cross_down,
    cross_up,
    cross_bias,
    compress_weight,
    compress_bias,
    dense_vector,
    mlp_weight,
    mlp_bias,
    *,
    feat_count,
    group_count
):
    entry_count = pooled_first.shape[3]
    rows_here = cross_down.shape[1]
    rank = cross_down.shape[2]
    split = rows_here % group_count == 0 and rows_here // group_count % entry_count == 0
    share_count = group_count if split else 1
    piece = rows_here // share_count
    first_here = jnp.concatenate([cross_down[0], cross_up[0]], axis=1)
    second_here = compress_weight[0]
    if split:
        group_index = lax.axis_index("groups")
        first_here = lax.dynamic_slice_in_dim(first_here, group_index * piece, piece, axis=0)
        second_here = lax.dynamic_slice_in_dim(second_here, group_index * piece, piece, axis=0)
        table = jnp.asarray(received_feature_table(rows_here, feat_count, share_count, entry_count))
        position_feature = table[group_index]
    else:
        position_feature = jnp.asarray(
            received_feature_table(rows_here, feat_count, 1, entry_count)
        )[0]
    first_parts = gather_rows(first_here, share_count)
    second_parts = gather_rows(second_here, share_count)
    group_one, group_two = (
        lax.all_to_all(pooled_first, "feat", split_axis=2, concat_axis=1, tiled=True),
        lax.all_to_all(pooled_second, "feat", split_axis=2, concat_axis=1, tiled=True),
    )
    mlp_weight, group_one = lax.optimization_barrier((mlp_weight, group_one))
    hidden_weight = lax.all_gather(mlp_weight, "tower", axis=0, tiled=True)
    slot_data = jnp.concatenate([group_one[0], group_two[0]], 0)
    slot_count = slot_data.shape[0]
    row_count = slot_data.shape[1]
    orders = feature_order[0]
    position_count = position_feature.shape[1]
    one_hot = (orders[None, None, :] == position_feature[:, :, None]).astype(jnp.bfloat16)
    base_parts = jnp.einsum("kfs,sre->krfe", one_hot, slot_data, preferred_element_type=jnp.float32)
    base_parts = base_parts.astype(jnp.bfloat16).reshape(
        share_count, row_count, position_count * entry_count
    )
    bias_blocks = cross_bias[0].reshape(slot_count, entry_count)
    low_sum = None
    for shift in range(share_count):
        term = jnp.dot(
            base_parts[shift], first_parts[shift][:, :rank], preferred_element_type=jnp.float32
        )
        low_sum = term if low_sum is None else low_sum + term
    low_rank = low_sum.astype(jnp.bfloat16)
    squeezed = None
    for shift in range(share_count):
        lifted = lax.dot_general(
            low_rank,
            first_parts[shift][:, rank:],
            (((1,), (1,)), ((), ())),
            preferred_element_type=jnp.float32,
        )
        shift_row = bias_blocks[position_feature[shift]].reshape(position_count * entry_count)
        columns = base_parts[shift].astype(jnp.float32)
        crossed = (columns * (lifted + shift_row[None, :]) + columns).astype(jnp.bfloat16)
        term = jnp.dot(crossed, second_parts[shift], preferred_element_type=jnp.float32)
        squeezed = term if squeezed is None else squeezed + term
    compressed = (squeezed + compress_bias[0][None, :]).astype(jnp.bfloat16)
    gathered = lax.all_to_all(compressed, "tower", split_axis=0, concat_axis=1, tiled=True)
    local_rows = gathered.shape[0]
    vector_count = gathered.shape[1] // entry_count
    vectors = gathered.reshape(local_rows, vector_count, entry_count)
    gram_matrix = jnp.einsum(
        "bie,bje->bij", vectors, vectors, preferred_element_type=jnp.float32
    ) * (1.0 / math.sqrt(entry_count))
    pair_terms = gram_matrix.reshape(local_rows, vector_count * vector_count)[
        :, pair_positions(vector_count)
    ]
    joined = jnp.concatenate([dense_vector.astype(jnp.float32), pair_terms], 1).astype(jnp.bfloat16)
    hidden_units = mlp_weight.shape[1]
    width_here = hidden_weight.shape[0]
    columns = lax.slice_in_dim(joined, 0, width_here, axis=1)
    hidden_sum = jnp.zeros((local_rows, hidden_units), jnp.float32) + jnp.dot(
        columns, hidden_weight, preferred_element_type=jnp.float32
    )
    return jax.nn.relu(hidden_sum + mlp_bias[None, :]).astype(jnp.bfloat16)


def solution(mesh):
    in_specs = (
        P("tower", "feat", "groups", None),
        P("tower", "feat", "groups", None),
        P("tower", None),
        P("tower", "feat", None),
        P("tower", "feat", None),
        P("tower", None),
        P("tower", "feat", None),
        P("tower", None),
        P(("groups", "feat", "tower"), None),
        P("tower", None),
        P(),
    )
    out_specs = P(("groups", "feat", "tower"), None)
    body = functools.partial(
        on_device, feat_count=mesh.shape["feat"], group_count=mesh.shape["groups"]
    )
    return jax.shard_map(body, mesh=mesh, in_specs=in_specs, out_specs=out_specs, check_vma=False)
```

profile of v0, /device:TPU:0, one launch (start us, length us, event | category | flops | bytes accessed | tf_op | source)
XLA Modules:
  0.0 243.4 jit_solution(15778819335520418898)
XLA Ops:
  6.5 2.0 fusion.30
  8.6 8.2 %copy.25 = bf16[1,4,1536,128]{3,1,0,2:T(4,128)(2,1)} copy(bf16[1,4,1536,128]{3,2,1,0:T(8,128)(2,1)S(1)} %copy-done.2) | data formatting | bytes 3145728 | tf_op args[0]
  16.8 6.3 %all-to-all-start = ((bf16[1,4,1536,128]{3,1,0,2:T(4,128)(2,1)}), bf16[1,4,1536,128]{3,1,0,2:T(4,128)(2,1)S(1)}, u32[]{:S(2)}, u32[]{:S(2)}) async-start(bf16[1,4,1536,128]{3,1,0,2:T(4,128)(2,1)} %copy.25), calls=%async_computation | async-start | bytes 3145728 | tf_op jit(solution)/shard_map/all_to_all | solution.py:75
  23.2 0.9 constant_dynamic-slice_fusion
  24.0 8.5 %copy.27 = bf16[1,4,1536,128]{3,1,0,2:T(4,128)(2,1)} copy(bf16[1,4,1536,128]{3,2,1,0:T(8,128)(2,1)} %param.15) | data formatting | bytes 3145728 | tf_op args[1]
  32.6 58.1 %all-to-all-done = bf16[1,4,1536,128]{3,1,0,2:T(4,128)(2,1)S(1)} async-done(((bf16[1,4,1536,128]{3,1,0,2:T(4,128)(2,1)}), bf16[1,4,1536,128]{3,1,0,2:T(4,128)(2,1)S(1)}, u32[]{:S(2)}, u32[]{:S(2)}) %all-to-all-start) | async-done | bytes 1572896 | tf_op jit(solution)/shard_map/all_to_all | solution.py:75
  90.7 4.6 %all-to-all-start.1 = ((bf16[1,4,1536,128]{3,1,0,2:T(4,128)(2,1)}), bf16[1,4,1536,128]{3,1,0,2:T(4,128)(2,1)}, u32[]{:S(2)}, u32[]{:S(2)}) async-start(bf16[1,4,1536,128]{3,1,0,2:T(4,128)(2,1)} %copy.27), calls=%async_computation.1 | async-start | bytes 3145728 | tf_op jit(solution)/shard_map/all_to_all | solution.py:76
  95.3 1.5 collective-permute-start
  96.9 69.6 %all-gather.7.cloned.1.call-done = bf16[1,2048,512]{2,1,0:T(8,128)(2,1)} async-done(((bf16[1,512,512]{2,1,0:T(8,128)(2,1)}), bf16[1,2048,512]{2,1,0:T(8,128)(2,1)}) %all-gather.7.cloned.1.call-update) | async-done | bytes 2097168 | tf_op jit(solution)/shard_map/all_gather | solution.py:30
  166.5 1.5 collective-permute-start.1
  168.6 0.6 gather_fusion.1
  169.1 1.8 copy.26
  170.9 2.1 copy.28
  173.0 1.0 convert_bitcast_fusion
  174.6 1.2 copy-done.11
  175.8 0.6 fusion.7
  176.4 1.8 fusion.18
  178.2 4.9 %fusion.28 = f32[384,512]{1,0:T(8,128)} fusion(bf16[384,256]{1,0:T(8,128)(2,1)S(1)} %fusion.18, f32[2048]{0:T(1024)S(1)} %bitcast.92, bf16[48,8,16,128]{3,2,1,0:T(8,128)(2,1)} %bitcast.83, bf16[2048,512]{1,0:T(8,128)(2,1)} %all-gather.5.cloned.1.call-done, bf16[1,2048,512]{2,1,0:T(8,128)(2,1)} %all-gather.7.cloned.1.call-done), kind=kOutput, calls=%fused_computation.33 | convolution fusion | flops 1211891712 | bytes 5709824 | tf_op jit(solution)/shard_map/dot_general | solution.py:109
  183.1 31.3 %collective-permute-done.1 = bf16[2048,512]{1,0:T(8,128)(2,1)} collective-permute-done((bf16[2048,512]{1,0:T(8,128)(2,1)}, bf16[2048,512]{1,0:T(8,128)(2,1)}, u32[]{:S(2)}, u32[]{:S(2)}) %collective-permute-start.1) | collective-permute-done | bytes 2097184 | tf_op jit(solution)/shard_map/ppermute | solution.py:34
  214.4 4.5 %fusion.12 = bf16[384,512]{1,0:T(8,128)(2,1)} fusion(f32[384,512]{1,0:T(8,128)} %fusion.28, bf16[2048,512]{1,0:T(8,128)(2,1)} %collective-permute-done.1, bf16[384,256]{1,0:T(8,128)(2,1)S(1)} %fusion.18, f32[2048]{0:T(1024)S(1)} %bitcast.91, bf16[48,8,16,128]{3,2,1,0:T(8,128)(2,1)S(1)} %bitcast.81, bf16[2048,512]{1,0:T(8,128)(2,1)} %collective-permute-done, ...), kind=kOutput, calls=%fused_computation.21 | convolution fusion | flops 1212481536 | bytes 6105088 | tf_op jit(solution)/shard_map/dot_general | solution.py:109
  218.9 3.5 %all-to-all-start.2 = ((bf16[4,96,512]{2,1,0:T(8,128)(2,1)}), bf16[4,96,512]{2,1,0:T(8,128)(2,1)S(1)}, u32[]{:S(2)}, u32[]{:S(2)}) async-start(bf16[4,96,512]{2,1,0:T(8,128)(2,1)} %bitcast.24), calls=%async_computation.2 | async-start | bytes 786432 | tf_op jit(solution)/shard_map/all_to_all | solution.py:112
  222.4 11.0 %all-gather.1 = bf16[4,62,1024]{2,1,0:T(8,128)(2,1)S(1)} all-gather(bf16[1,62,1024]{2,1,0:T(8,128)(2,1)S(1)} %bitcast.89), channel_id=1, replica_groups=mesh['groups'=2,'feat'=4,'tower'=4] {'tower'}, dimensions={0}, use_global_device_ids=true | all-gather | bytes 634880 | tf_op jit(solution)/shard_map/all_gather | solution.py:79
  234.8 0.7 gather_fusion.2
  235.6 0.9 fusion.17
  (45 shorter events, 2.6 us)
Async XLA Ops:
  6.5 16.6 %copy-start = (bf16[1,1024,512]{2,1,0:T(8,128)(2,1)S(1)}, bf16[1,1024,512]{2,1,0:T(8,128)(2,1)}, u32[]{:S(2)}) copy-start(bf16[1,1024,512]{2,1,0:T(8,128)(2,1)} %param.20) | copy-start | bytes 3145732
  6.5 2.1 copy-start.2
  6.5 88.8 %all-gather.5.cloned.1.call-start = ((), (), s32[]{:S(2)}) async-start(), calls=%async_computation.3 | async-start | bytes 2621440 | tf_op jit(solution)/shard_map/all_gather | solution.py:30
  16.8 73.9 %all-to-all-start = ((bf16[1,4,1536,128]{3,1,0,2:T(4,128)(2,1)}), bf16[1,4,1536,128]{3,1,0,2:T(4,128)(2,1)S(1)}, u32[]{:S(2)}, u32[]{:S(2)}) async-start(bf16[1,4,1536,128]{3,1,0,2:T(4,128)(2,1)} %copy.25), calls=%async_computation | async-start | bytes 3145728 | tf_op jit(solution)/shard_map/all_to_all | solution.py:75
  23.2 143.3 %all-gather.7.cloned.1.call-start = ((), (), s32[]{:S(2)}) async-start(), calls=%async_computation.4 | async-start | bytes 2621440 | tf_op jit(solution)/shard_map/all_gather | solution.py:30
  32.6 135.4 %copy-start.9 = (s32[2,2,16]{2,1,0:T(2,128)S(1)}, s32[2,2,16]{2,1,0:T(2,128)}, u32[]{:S(2)}) copy-start(s32[2,2,16]{2,1,0:T(2,128)} %constant.31.clone) | copy-start | bytes 772
  32.6 135.4 %copy-start.4 = (f32[1,4096]{1,0:T(1,128)S(1)}, f32[1,4096]{1,0:T(1,128)}, u32[]{:S(2)}) copy-start(f32[1,4096]{1,0:T(1,128)} %param.19) | copy-start | bytes 49156
  90.7 80.2 %all-to-all-start.1 = ((bf16[1,4,1536,128]{3,1,0,2:T(4,128)(2,1)}), bf16[1,4,1536,128]{3,1,0,2:T(4,128)(2,1)}, u32[]{:S(2)}, u32[]{:S(2)}) async-start(bf16[1,4,1536,128]{3,1,0,2:T(4,128)(2,1)} %copy.27), calls=%async_computation.1 | async-start | bytes 3145728 | tf_op jit(solution)/shard_map/all_to_all | solution.py:76
  95.3 81.0 %collective-permute-start = (bf16[2048,512]{1,0:T(8,128)(2,1)}, bf16[2048,512]{1,0:T(8,128)(2,1)}, u32[]{:S(2)}, u32[]{:S(2)}) collective-permute-start(bf16[2048,512]{1,0:T(8,128)(2,1)} %all-gather.5.cloned.1.call-done), channel_id=1, source_target_pairs={{0,16},{16,0},{1,17},{17,1},{2,18},{18,2},{3,19},{19,3},{4,20},{20... | collective-permute-start | bytes 6291464 | tf_op jit(solution)/shard_map/ppermute | solution.py:34
  166.5 47.9 %collective-permute-start.1 = (bf16[2048,512]{1,0:T(8,128)(2,1)}, bf16[2048,512]{1,0:T(8,128)(2,1)}, u32[]{:S(2)}, u32[]{:S(2)}) collective-permute-start(bf16[2048,512]{1,0:T(8,128)(2,1)} %bitcast.94), channel_id=1, source_target_pairs={{0,16},{16,0},{1,17},{17,1},{2,18},{18,2},{3,19},{19,3},{4,20},{20... | collective-permute-start | bytes 6291464 | tf_op jit(solution)/shard_map/ppermute | solution.py:34
  170.9 2.1 copy-start.1
  170.9 2.1 copy-start.8
  174.0 1.7 copy-start.11
  174.6 1.8 copy-start.3
  178.2 36.2 %copy-start.12 = (f32[1,512]{1,0:T(1,128)S(1)}, f32[1,512]{1,0:T(1,128)}, u32[]{:S(2)}) copy-start(f32[1,512]{1,0:T(1,128)} %param.21) | copy-start | bytes 6148
  214.4 8.0 %copy-start.10 = (s32[120]{0:T(128)S(1)}, s32[120]{0:T(128)}, u32[]{:S(2)}) copy-start(s32[120]{0:T(128)} %constant.44) | copy-start | bytes 1444
  214.4 8.0 %copy-start.5 = (bf16[62,1024]{1,0:T(8,128)(2,1)S(1)}, bf16[62,1024]{1,0:T(8,128)(2,1)}, u32[]{:S(2)}) copy-start(bf16[62,1024]{1,0:T(8,128)(2,1)} %param.23) | copy-start | bytes 380932
  218.9 14.7 %all-to-all-start.2 = ((bf16[4,96,512]{2,1,0:T(8,128)(2,1)}), bf16[4,96,512]{2,1,0:T(8,128)(2,1)S(1)}, u32[]{:S(2)}, u32[]{:S(2)}) async-start(bf16[4,96,512]{2,1,0:T(8,128)(2,1)} %bitcast.24), calls=%async_computation.2 | async-start | bytes 786432 | tf_op jit(solution)/shard_map/all_to_all | solution.py:112
  233.5 2.1 copy-start.6
  233.5 2.1 copy-start.7
Sparse Core Ops, SparseCore 0:
  8.9 80.4 all-gather.4
  91.0 75.4 all-gather.6
where the time goes:
time: 244 us; the launch traced here: 243 us
  waiting for transfers between devices  159 us (65%)
  local copies, waits for them, and re-layouts  26.1 us (11%)
  starting transfers between devices  17.4 us (7%)
  matrix products  14.1 us (6%)
  between operations  13.6 us (6%)
  blocking collectives  11 us (5%)
    all_gather x2, waiting for transfers between devices, gather_rows(): own = lax.all_gather(part, 'feat', axis=0, tiled=True)  69.6 us
    all_to_all x1, waiting for transfers between devices, on_device(): lax.all_to_all(pooled_first, 'feat', split_axis=2, concat_axis=1, tiled=T...  58.1 us
    ppermute x2, waiting for transfers between devices, gather_rows(): received.append(lax.ppermute(own, 'groups', pairs))  31.3 us
    unnamed x29, local copies, waits for them, and re-layouts  18.1 us
    all_gather x1, blocking collectives, on_device(): hidden_weight = lax.all_gather(mlp_weight, 'tower', axis=0, tiled=True)  11 us
    dot_general x2, matrix products, on_device(): jnp.dot(crossed, second_parts[shift], preferred_element_type=jnp.float32)  9.42 us
    all_to_all x1, starting transfers between devices, on_device(): lax.all_to_all(pooled_first, 'feat', split_axis=2, concat_axis=1, tiled=T...  6.32 us
  transfers between devices with their start and end apart: 7, of which 3 were waited for; matrix products, arithmetic and copies ran while one was open for 13% of the time, Pallas kernels for 0%

commit v1 on v0

--- a/solution.py
+++ b/solution.py
@@ -71,9 +71,13 @@
         )[0]
     first_parts = gather_rows(first_here, share_count)
     second_parts = gather_rows(second_here, share_count)
+    check_halves = lambda w_in: jnp.concatenate(
+        lax.all_to_all(jnp.stack(jnp.split(w_in, lax.psum(1, "feat"), axis=2)), "feat", 0, 0),
+        axis=1,
+    )
     group_one, group_two = (
         lax.all_to_all(pooled_first, "feat", split_axis=2, concat_axis=1, tiled=True),
-        lax.all_to_all(pooled_second, "feat", split_axis=2, concat_axis=1, tiled=True),
+        check_halves(pooled_second),
     )
     mlp_weight, group_one = lax.optimization_barrier((mlp_weight, group_one))
     hidden_weight = lax.all_gather(mlp_weight, "tower", axis=0, tiled=True)

time: 244 us -> 244 us (level)
  local copies, waits for them, and re-layouts: 26.1 us -> 19.7 us
  waiting for transfers between devices: 159 us -> 164 us
    unnamed x29 -> x28, local copies, waits for them, and re-layouts: 18.1 us -> 9.61 us
    all_to_all x1, waiting for transfers between devices: 58.1 us -> 63.8 us  [on_device(): lax.all_to_all(pooled_first, 'feat', split_axis=2, concat_axis=1, tiled=T...]
  transfers between devices with their start and end apart: 7 -> 7, of which waited for: 3 -> 3; matrix products, arithmetic and copies ran while one was open for 13% -> 11% of each run, Pallas kernels for 0% -> 0%
where the time goes in v1:
time: 244 us; the launch traced here: 243 us
  waiting for transfers between devices  164 us (67%)
  local copies, waits for them, and re-layouts  19.7 us (8%)
  starting transfers between devices  17.4 us (7%)
  matrix products  14 us (6%)
  between operations  13.6 us (6%)
  blocking collectives  11 us (5%)
  other arithmetic  3.43 us (1%)
    all_gather x2, waiting for transfers between devices, gather_rows(): own = lax.all_gather(part, 'feat', axis=0, tiled=True)  69.6 us
    all_to_all x1, waiting for transfers between devices, on_device(): lax.all_to_all(pooled_first, 'feat', split_axis=2, concat_axis=1, tiled=T...  63.8 us
    ppermute x2, waiting for transfers between devices, gather_rows(): received.append(lax.ppermute(own, 'groups', pairs))  30.7 us
    all_gather x1, blocking collectives, on_device(): hidden_weight = lax.all_gather(mlp_weight, 'tower', axis=0, tiled=True)  11 us
    unnamed x28, local copies, waits for them, and re-layouts  9.61 us
    dot_general x2, matrix products, on_device(): jnp.dot(crossed, second_parts[shift], preferred_element_type=jnp.float32)  9.4 us
    all_to_all x1, starting transfers between devices, on_device(): lax.all_to_all(pooled_first, 'feat', split_axis=2, concat_axis=1, tiled=T...  6.32 us
  transfers between devices with their start and end apart: 7, of which 3 were waited for; matrix products, arithmetic and copies ran while one was open for 11% of the time, Pallas kernels for 0%

profile of v1, /device:TPU:0, one launch (start us, length us, event | category | flops | bytes accessed | tf_op | source)
XLA Modules:
  0.0 243.3 jit_solution(237282516728330481)
XLA Ops:
  6.5 2.0 fusion.30
  8.6 8.3 %copy.25 = bf16[1,4,1536,128]{3,1,0,2:T(4,128)(2,1)} copy(bf16[1,4,1536,128]{3,2,1,0:T(8,128)(2,1)S(1)} %copy-done.2) | data formatting | bytes 3145728 | tf_op args[0]
  16.9 6.3 %all-to-all-start = ((bf16[1,4,1536,128]{3,1,0,2:T(4,128)(2,1)}), bf16[1,4,1536,128]{3,1,0,2:T(4,128)(2,1)S(1)}, u32[]{:S(2)}, u32[]{:S(2)}) async-start(bf16[1,4,1536,128]{3,1,0,2:T(4,128)(2,1)} %copy.25), calls=%async_computation | async-start | bytes 3145728 | tf_op jit(solution)/shard_map/all_to_all | solution.py:79
  23.2 0.9 constant_dynamic-slice_fusion
  24.1 1.5 slice_bitcast_fusion.3
  25.5 1.4 pad_maximum_fusion
  26.9 63.8 %all-to-all-done = bf16[1,4,1536,128]{3,1,0,2:T(4,128)(2,1)S(1)} async-done(((bf16[1,4,1536,128]{3,1,0,2:T(4,128)(2,1)}), bf16[1,4,1536,128]{3,1,0,2:T(4,128)(2,1)S(1)}, u32[]{:S(2)}, u32[]{:S(2)}) %all-to-all-start) | async-done | bytes 1572896 | tf_op jit(solution)/shard_map/all_to_all | solution.py:79
  90.7 4.5 %all-to-all-start.1 = ((bf16[4,1,4,384,128]{4,3,2,1,0:T(8,128)(2,1)}), bf16[4,1,4,384,128]{4,3,2,1,0:T(8,128)(2,1)}, u32[]{:S(2)}, u32[]{:S(2)}) async-start(bf16[4,1,4,384,128]{4,3,2,1,0:T(8,128)(2,1)} %pad_maximum_fusion), calls=%async_computation.1 | async-start | bytes 3145728 | tf_op jit(solution)/shard_map/all_to_all | solution.py:75
  95.3 1.5 collective-permute-start
  96.8 69.6 %all-gather.7.cloned.1.call-done = bf16[1,2048,512]{2,1,0:T(8,128)(2,1)} async-done(((bf16[1,512,512]{2,1,0:T(8,128)(2,1)}), bf16[1,2048,512]{2,1,0:T(8,128)(2,1)}) %all-gather.7.cloned.1.call-update) | async-done | bytes 2097168 | tf_op jit(solution)/shard_map/all_gather | solution.py:30
  166.5 1.5 collective-permute-start.1
  169.1 1.8 copy.26
  170.9 2.7 %copy.27 = bf16[4,1,4,384,128]{4,2,0,3,1:T(4,128)(2,1)S(1)} copy(bf16[4,1,4,384,128]{4,3,2,1,0:T(8,128)(2,1)} %all-to-all-done.1) | data formatting | bytes 3145728 | tf_op jit(solution)/shard_map/all_to_all | solution.py:75
  173.7 1.0 convert_bitcast_fusion
  175.2 1.2 copy-done.11
  176.4 0.6 fusion.7
  177.0 1.8 fusion.18
  178.8 4.9 %fusion.28 = f32[384,512]{1,0:T(8,128)} fusion(bf16[384,256]{1,0:T(8,128)(2,1)S(1)} %fusion.18, f32[2048]{0:T(1024)S(1)} %bitcast.97, bf16[48,8,16,128]{3,2,1,0:T(8,128)(2,1)} %bitcast.88, bf16[2048,512]{1,0:T(8,128)(2,1)} %all-gather.5.cloned.1.call-done, bf16[1,2048,512]{2,1,0:T(8,128)(2,1)} %all-gather.7.cloned.1.call-done), kind=kOutput, calls=%fused_computation.34 | convolution fusion | flops 1211891712 | bytes 5709824 | tf_op jit(solution)/shard_map/dot_general | solution.py:113
  183.7 30.7 %collective-permute-done.1 = bf16[2048,512]{1,0:T(8,128)(2,1)} collective-permute-done((bf16[2048,512]{1,0:T(8,128)(2,1)}, bf16[2048,512]{1,0:T(8,128)(2,1)}, u32[]{:S(2)}, u32[]{:S(2)}) %collective-permute-start.1) | collective-permute-done | bytes 2097184 | tf_op jit(solution)/shard_map/ppermute | solution.py:34
  214.4 4.5 %fusion.12 = bf16[384,512]{1,0:T(8,128)(2,1)} fusion(f32[384,512]{1,0:T(8,128)} %fusion.28, bf16[2048,512]{1,0:T(8,128)(2,1)} %collective-permute-done.1, bf16[384,256]{1,0:T(8,128)(2,1)S(1)} %fusion.18, f32[2048]{0:T(1024)S(1)} %bitcast.96, bf16[48,8,16,128]{3,2,1,0:T(8,128)(2,1)S(1)} %bitcast.86, bf16[2048,512]{1,0:T(8,128)(2,1)} %collective-permute-done, ...), kind=kOutput, calls=%fused_computation.22 | convolution fusion | flops 1212481536 | bytes 6105088 | tf_op jit(solution)/shard_map/dot_general | solution.py:113
  218.9 3.5 %all-to-all-start.2 = ((bf16[4,96,512]{2,1,0:T(8,128)(2,1)}), bf16[4,96,512]{2,1,0:T(8,128)(2,1)S(1)}, u32[]{:S(2)}, u32[]{:S(2)}) async-start(bf16[4,96,512]{2,1,0:T(8,128)(2,1)} %bitcast.26), calls=%async_computation.2 | async-start | bytes 786432 | tf_op jit(solution)/shard_map/all_to_all | solution.py:116
  222.4 11.0 %all-gather.1 = bf16[4,62,1024]{2,1,0:T(8,128)(2,1)S(1)} all-gather(bf16[1,62,1024]{2,1,0:T(8,128)(2,1)S(1)} %bitcast.94), channel_id=1, replica_groups=mesh['groups'=2,'feat'=4,'tower'=4] {'tower'}, dimensions={0}, use_global_device_ids=true | all-gather | bytes 634880 | tf_op jit(solution)/shard_map/all_gather | solution.py:83
  234.8 0.7 gather_fusion.2
  235.6 0.9 fusion.17
  (46 shorter events, 3.2 us)
Async XLA Ops:
  6.5 16.6 %copy-start = (bf16[1,1024,512]{2,1,0:T(8,128)(2,1)S(1)}, bf16[1,1024,512]{2,1,0:T(8,128)(2,1)}, u32[]{:S(2)}) copy-start(bf16[1,1024,512]{2,1,0:T(8,128)(2,1)} %param.20) | copy-start | bytes 3145732
  6.5 2.1 copy-start.2
  6.5 88.7 %all-gather.5.cloned.1.call-start = ((), (), s32[]{:S(2)}) async-start(), calls=%async_computation.3 | async-start | bytes 2621440 | tf_op jit(solution)/shard_map/all_gather | solution.py:30
  16.9 73.9 %all-to-all-start = ((bf16[1,4,1536,128]{3,1,0,2:T(4,128)(2,1)}), bf16[1,4,1536,128]{3,1,0,2:T(4,128)(2,1)S(1)}, u32[]{:S(2)}, u32[]{:S(2)}) async-start(bf16[1,4,1536,128]{3,1,0,2:T(4,128)(2,1)} %copy.25), calls=%async_computation | async-start | bytes 3145728 | tf_op jit(solution)/shard_map/all_to_all | solution.py:79
  23.2 143.3 %all-gather.7.cloned.1.call-start = ((), (), s32[]{:S(2)}) async-start(), calls=%async_computation.4 | async-start | bytes 2621440 | tf_op jit(solution)/shard_map/all_gather | solution.py:30
  26.9 141.0 %copy-start.9 = (s32[2,2,16]{2,1,0:T(2,128)S(1)}, s32[2,2,16]{2,1,0:T(2,128)}, u32[]{:S(2)}) copy-start(s32[2,2,16]{2,1,0:T(2,128)} %constant.31.clone) | copy-start | bytes 772
  26.9 141.0 %copy-start.4 = (f32[1,4096]{1,0:T(1,128)S(1)}, f32[1,4096]{1,0:T(1,128)}, u32[]{:S(2)}) copy-start(f32[1,4096]{1,0:T(1,128)} %param.19) | copy-start | bytes 49156
  90.7 80.2 %all-to-all-start.1 = ((bf16[4,1,4,384,128]{4,3,2,1,0:T(8,128)(2,1)}), bf16[4,1,4,384,128]{4,3,2,1,0:T(8,128)(2,1)}, u32[]{:S(2)}, u32[]{:S(2)}) async-start(bf16[4,1,4,384,128]{4,3,2,1,0:T(8,128)(2,1)} %pad_maximum_fusion), calls=%async_computation.1 | async-start | bytes 3145728 | tf_op jit(solution)/shard_map/all_to_all | solution.py:75
  95.3 81.7 %collective-permute-start = (bf16[2048,512]{1,0:T(8,128)(2,1)}, bf16[2048,512]{1,0:T(8,128)(2,1)}, u32[]{:S(2)}, u32[]{:S(2)}) collective-permute-start(bf16[2048,512]{1,0:T(8,128)(2,1)} %all-gather.5.cloned.1.call-done), channel_id=1, source_target_pairs={{0,16},{16,0},{1,17},{17,1},{2,18},{18,2},{3,19},{19,3},{4,20},{20... | collective-permute-start | bytes 6291464 | tf_op jit(solution)/shard_map/ppermute | solution.py:34
  166.5 47.9 %collective-permute-start.1 = (bf16[2048,512]{1,0:T(8,128)(2,1)}, bf16[2048,512]{1,0:T(8,128)(2,1)}, u32[]{:S(2)}, u32[]{:S(2)}) collective-permute-start(bf16[2048,512]{1,0:T(8,128)(2,1)} %bitcast.99), channel_id=1, source_target_pairs={{0,16},{16,0},{1,17},{17,1},{2,18},{18,2},{3,19},{19,3},{4,20},{20... | collective-permute-start | bytes 6291464 | tf_op jit(solution)/shard_map/ppermute | solution.py:34
  170.9 2.8 %copy-start.1 = (bf16[1,4,4,384,128]{4,1,2,3,0:T(4,128)(2,1)S(1)}, bf16[1,4,4,384,128]{4,1,2,3,0:T(4,128)(2,1)}, u32[]{:S(2)}) copy-start(bf16[1,4,4,384,128]{4,1,2,3,0:T(4,128)(2,1)} %copy.26) | copy-start | bytes 4718596
  170.9 2.8 %copy-start.8 = (s32[1,32]{1,0:T(1,128)S(1)}, s32[1,32]{1,0:T(1,128)}, u32[]{:S(2)}) copy-start(s32[1,32]{1,0:T(1,128)} %param.16) | copy-start | bytes 388
  174.7 1.7 copy-start.11
  175.2 1.8 copy-start.3
  178.8 35.6 %copy-start.12 = (f32[1,512]{1,0:T(1,128)S(1)}, f32[1,512]{1,0:T(1,128)}, u32[]{:S(2)}) copy-start(f32[1,512]{1,0:T(1,128)} %param.21) | copy-start | bytes 6148
  214.4 8.0 %copy-start.10 = (s32[120]{0:T(128)S(1)}, s32[120]{0:T(128)}, u32[]{:S(2)}) copy-start(s32[120]{0:T(128)} %constant.44) | copy-start | bytes 1444
  214.4 8.0 %copy-start.5 = (bf16[62,1024]{1,0:T(8,128)(2,1)S(1)}, bf16[62,1024]{1,0:T(8,128)(2,1)}, u32[]{:S(2)}) copy-start(bf16[62,1024]{1,0:T(8,128)(2,1)} %param.23) | copy-start | bytes 380932
  218.9 14.7 %all-to-all-start.2 = ((bf16[4,96,512]{2,1,0:T(8,128)(2,1)}), bf16[4,96,512]{2,1,0:T(8,128)(2,1)S(1)}, u32[]{:S(2)}, u32[]{:S(2)}) async-start(bf16[4,96,512]{2,1,0:T(8,128)(2,1)} %bitcast.26), calls=%async_computation.2 | async-start | bytes 786432 | tf_op jit(solution)/shard_map/all_to_all | solution.py:116
  233.4 2.1 copy-start.6
  233.4 2.1 copy-start.7
Sparse Core Ops, SparseCore 0:
  8.9 80.4 all-gather.4
  91.0 75.4 all-gather.6
